TPU v7x, 256 devices: a whole 4x4x8 slice. The times are simulated.
256 devices in a mesh: sec: 2 (over y_lo), dp: 8 (over x, y_hi), seq: 16 (over z, core).
Axes of the slice: x: 4, y: 4 (y_hi: 2, y_lo: 2; y = y_hi * 2 + y_lo), z: 8, core: 2. Of those that a mesh axis runs over, the one named last changes fastest.
Arguments:
- hidden: bfloat16 [256, 128, 2560], P(('sec', 'dp', 'seq')), may hold values from -24 to 24
- cond_shift: bfloat16 [256, 2560], P(('sec', 'dp', 'seq')), may hold values from -0.3125 to 0.3125
- cond_scale: bfloat16 [256, 2560], P(('sec', 'dp', 'seq')), may hold values from -1.75 to 1.75
- noisy: bfloat16 [256, 128, 256], P(('sec', 'dp', 'seq')), may hold values from -6 to 6
- noise_level: float32 [256], P(('sec', 'dp', 'seq')), may hold values from 0.2 to 1
- w_out: bfloat16 [2560, 256], replicated, may hold values from -0.125 to 0.125
- w_embed: bfloat16 [256, 2048], replicated, may hold values from -0.375 to 0.375
- w_root: bfloat16 [2, 2048], replicated, may hold values from -0.03125 to 0.03125
- w_qkv: bfloat16 [3, 2048, 2048], P(None, None, 'seq'), may hold values from -0.125 to 0.125
- w_proj: bfloat16 [2048, 512], P('seq'), may hold values from -0.125 to 0.125
- text_table: bfloat16 [49408, 512], P('seq'), may hold values from -6 to 6
- text_ids: int32 [32, 32], replicated, may hold values from 0 to 49407
- prompt_index: int32 [256], P(('sec', 'dp')), may hold values from 0 to 31
- reward_weight: float32 [256], P(('sec', 'dp')), may hold values from 1000 to 4000
Outputs:
- rewards: float32 [256], P(('sec', 'dp'))
- grad_w_out: float32 [2560, 256], P('seq')
- grad_hidden: bfloat16 [256, 128, 2560], P(('sec', 'dp', 'seq'))
All inputs are finite; a program needn't handle non-finite values.
Results may differ from a plain program's by a relative error of at most 0.017.
The roundings to bfloat16 on the way count: a program that leaves them out, or rounds other values in their place, can miss the bound.
Values may be sent and summed in bfloat16 or wider, within the bound.
No kernel may reach another device: no remote copies, remote signals or barrier semaphores. Data moves between devices by JAX's collectives and lax.ppermute only.
A program may use at most 128 MiB of HBM per device.

v0:
```python
import jax
import jax.numpy as jnp
from jax import lax
from jax.sharding import PartitionSpec as P

D_REW = 2048
HEADS = 16
PROMPTS = 32
normalizing_sharpness = 10.0
epsilon = 1e-06
highest = lax.Precision.HIGHEST


def rotate(angle, first, second):
    cosine = jnp.cos(angle)
    sine_term = jnp.sin(angle)
    return (cosine * first + sine_term * second, cosine * second - sine_term * first)


def suffix(values):
    return jnp.sum(values, axis=1, keepdims=True) - jnp.cumsum(values, axis=1)


def local_path(motion):
    spin = motion[..., 0]
    theta = jnp.cumsum(spin, axis=1) - spin
    step_east, step_north = rotate(theta, motion[..., 1], motion[..., 2])
    path_east = jnp.cumsum(step_east, axis=1) - step_east
    path_north = jnp.cumsum(step_north, axis=1) - step_north
    return (theta, path_east, path_north)


def embed(motion, root_east, root_north, w_embed, root_rows):
    emb = jnp.einsum(
        "cfe,ed->cfd", motion.astype(jnp.bfloat16), w_embed, preferred_element_type=jnp.float32
    )
    emb = emb + root_east[..., None] * root_rows[0] + root_north[..., None] * root_rows[1]
    scale_rms = jnp.sqrt(jnp.mean(emb * emb, axis=-1, keepdims=True) + epsilon)
    return (emb / scale_rms, scale_rms)


def unit_rows(vectors):
    length = jnp.sqrt(jnp.sum(vectors * vectors, axis=-1, keepdims=True) + epsilon)
    return (vectors / length, length)


def norm_grad(grad, normed, scale_rms):
    return (grad - normed * jnp.mean(grad * normed, axis=-1, keepdims=True)) / scale_rms


def motion_grad(d_emb, normed_e, scale_rms, motion, theta, embed_rows, root_rows):
    d_unemb = norm_grad(d_emb, normed_e, scale_rms)
    d_embedded = jnp.einsum("cfd,ed->cfe", d_unemb, embed_rows, precision=highest)
    grad_east = suffix(jnp.sum(d_unemb * root_rows[0], axis=-1))
    grad_north = suffix(jnp.sum(d_unemb * root_rows[1], axis=-1))
    vel_east = motion[..., 1]
    vel_north = motion[..., 2]
    d_east, d_north = rotate(-theta, grad_east, grad_north)
    cosine = jnp.cos(theta)
    sine_term = jnp.sin(theta)
    d_theta = grad_east * (cosine * vel_north - sine_term * vel_east) - grad_north * (
        cosine * vel_east + sine_term * vel_north
    )
    d_spin = suffix(d_theta)
    return d_embedded.at[..., 0].add(d_spin).at[..., 1].add(d_east).at[..., 2].add(d_north)


def local(
    hidden,
    cond_shift,
    cond_scale,
    noisy,
    noise_level,
    w_out,
    w_embed,
    w_root,
    w_qkv,
    w_proj,
    text_table,
    text_ids,
    prompt_index,
    reward_weight,
):
    clips_dev = hidden.shape[0]
    ways = lax.axis_size("seq")
    group = clips_dev * ways
    frames = hidden.shape[1]
    width_cols = w_qkv.shape[2]
    head_size = D_REW // HEADS
    heads_dev = width_cols // head_size
    root_rows = w_root.astype(jnp.float32)
    embed_rows = w_embed.astype(jnp.float32)
    vocab_rows = text_table.shape[0]
    local_ids = text_ids - lax.axis_index("seq") * vocab_rows
    inside = (local_ids >= 0) & (local_ids < vocab_rows)
    picked = jnp.take(text_table, jnp.clip(local_ids, 0, vocab_rows - 1), axis=0).astype(
        jnp.float32
    )
    text_part = jnp.sum(jnp.where(inside[..., None], picked, 0.0), axis=1)
    text_raw = lax.psum(text_part, "seq")
    text_unit, text_len = unit_rows(text_raw)
    hidden_f = hidden.astype(jnp.float32)
    centred = hidden_f - jnp.mean(hidden_f, axis=-1, keepdims=True)
    inv_std = lax.rsqrt(jnp.mean(centred * centred, axis=-1, keepdims=True) + epsilon)
    normed_h = centred * inv_std
    gain = 1.0 + cond_scale.astype(jnp.float32)[:, None, :]
    modulated = (normed_h * gain + cond_shift.astype(jnp.float32)[:, None, :]).astype(jnp.bfloat16)
    eps_pred = jnp.einsum("cfd,de->cfe", modulated, w_out, preferred_element_type=jnp.float32)
    level = noise_level[:, None, None]
    x_clean = noisy.astype(jnp.float32) - level * eps_pred
    theta, path_east, path_north = local_path(x_clean)
    normed_e, scale_rms = embed(x_clean, path_east, path_north, w_embed, root_rows)
    projected = jnp.einsum(
        "cfd,jdk->cfjk",
        lax.all_gather(normed_e.astype(jnp.bfloat16), "seq", axis=0, tiled=True),
        w_qkv,
        preferred_element_type=jnp.float32,
    )
    projected = projected.reshape(group, frames, 3, heads_dev, head_size)
    query_unit, query_len = unit_rows(projected[:, :, 0])
    key_unit, key_len = unit_rows(projected[:, :, 1])
    asking_vectors_group = query_unit.astype(jnp.bfloat16)
    lookup_vectors_group = key_unit.astype(jnp.bfloat16)
    value_b = projected[:, :, 2].astype(jnp.bfloat16)
    similarity_table = normalizing_sharpness * jnp.einsum(
        "cfhd,cghd->chfg",
        asking_vectors_group,
        lookup_vectors_group,
        preferred_element_type=jnp.float32,
    )
    expo = jnp.exp(similarity_table)
    focus_probabilities = expo / jnp.sum(expo, axis=-1, keepdims=True)
    attention_b = focus_probabilities.astype(jnp.bfloat16)
    column_mass = jnp.sum(attention_b, axis=2, dtype=jnp.float32)
    value_f = value_b.astype(jnp.float32)
    pooled = jnp.einsum("chg,cghd->chd", column_mass, value_f, precision=highest)
    pooled_b = pooled.astype(jnp.bfloat16).reshape(group, width_cols)
    motion_part = jnp.dot(pooled_b, w_proj, preferred_element_type=jnp.float32)
    motion_emb = lax.psum(motion_part, "seq")
    choose = (prompt_index[:, None] == jnp.arange(PROMPTS)[None, :]).astype(jnp.float32)
    target = jnp.dot(choose, text_unit, precision=highest)
    emb_len = jnp.sqrt(jnp.sum(motion_emb * motion_emb, axis=-1) + epsilon)
    rewards = jnp.sum(motion_emb * target, axis=-1) / emb_len
    d_memb = (
        (-reward_weight)[:, None]
        * (target - rewards[:, None] * motion_emb / emb_len[:, None])
        / emb_len[:, None]
    )
    d_pooled = jnp.dot(d_memb, w_proj.astype(jnp.float32).T, precision=highest).reshape(
        group, heads_dev, head_size
    )
    reduction_dimension = jnp.einsum("chd,cghd->chg", d_pooled, value_f, precision=highest)
    d_value = jnp.transpose(column_mass, (0, 2, 1))[..., None] * d_pooled[:, None]
    pairwise_dot_similarity = jnp.sum(
        focus_probabilities * reduction_dimension[:, :, None, :], axis=-1, keepdims=True
    )
    similarity_derivative = (
        normalizing_sharpness
        * focus_probabilities
        * (reduction_dimension[:, :, None, :] - pairwise_dot_similarity)
    ).astype(jnp.bfloat16)
    d_qu = jnp.einsum(
        "chfg,cghd->cfhd",
        similarity_derivative,
        lookup_vectors_group,
        preferred_element_type=jnp.float32,
    )
    d_ku = jnp.einsum(
        "chfg,cfhd->cghd",
        similarity_derivative,
        asking_vectors_group,
        preferred_element_type=jnp.float32,
    )
    d_query = (d_qu - query_unit * jnp.sum(query_unit * d_qu, axis=-1, keepdims=True)) / query_len
    d_key = (d_ku - key_unit * jnp.sum(key_unit * d_ku, axis=-1, keepdims=True)) / key_len
    d_proj = (
        jnp.stack([d_query, d_key, d_value], axis=2)
        .astype(jnp.bfloat16)
        .reshape(group, frames, 3, width_cols)
    )
    d_emb = lax.psum_scatter(
        jnp.einsum("cfjk,jdk->cfd", d_proj, w_qkv, preferred_element_type=jnp.float32),
        "seq",
        scatter_dimension=0,
        tiled=True,
    )
    d_motion = motion_grad(d_emb, normed_e, scale_rms, x_clean, theta, embed_rows, root_rows)
    d_eps_b = (-level * d_motion).astype(jnp.bfloat16)
    d_mod = jnp.einsum("cfe,de->cfd", d_eps_b, w_out, preferred_element_type=jnp.float32)
    d_norm = d_mod * gain
    grad_hidden = (
        inv_std
        * (
            d_norm
            - jnp.mean(d_norm, axis=-1, keepdims=True)
            - normed_h * jnp.mean(d_norm * normed_h, axis=-1, keepdims=True)
        )
    ).astype(jnp.bfloat16)
    rows_dev = w_out.shape[0] // ways
    grad_term = jnp.einsum("cfd,cfe->de", modulated, d_eps_b, preferred_element_type=jnp.float32)
    grad_total = lax.psum(grad_term, ("sec", "dp", "seq"))
    grad_w_out = lax.dynamic_slice_in_dim(grad_total, lax.axis_index("seq") * rows_dev, rows_dev, 0)
    return (rewards, grad_w_out, grad_hidden)


def solution(mesh):
    placed = (
        P(("sec", "dp", "seq"), None, None),
        P(("sec", "dp", "seq"), None),
        P(("sec", "dp", "seq"), None),
        P(("sec", "dp", "seq"), None, None),
        P(("sec", "dp", "seq")),
        P(),
        P(),
        P(),
        P(None, None, "seq"),
        P("seq", None),
        P("seq", None),
        P(),
        P(("sec", "dp")),
        P(("sec", "dp")),
    )
    return jax.shard_map(
        local,
        mesh=mesh,
        in_specs=placed,
        out_specs=(P(("sec", "dp")), P("seq", None), P(("sec", "dp", "seq"), None, None)),
        check_vma=False,
    )
```

profile of v0, /device:TPU:2, one launch (start us, length us, event | category | flops | bytes accessed | tf_op | source)
XLA Modules:
  0.0 640.3 jit_solution(5430359469314224564)
XLA Ops:
  7.2 0.9 compare_and_fusion
  8.2 0.9 copy-done
  9.1 5.1 gather_fusion
  14.2 2.3 select_reduce_fusion
  17.3 1.3 convert_reduce_fusion
  18.5 1.4 fusion.22
  20.0 0.6 fusion.77
  20.7 1.8 fusion.24
  22.5 0.8 slice_reduce_fusion.1
  23.8 0.5 copy-done.33
  25.1 0.6 subtract_reduce_fusion.1
  26.0 1.7 multiply_reduce_fusion.3
  27.8 0.9 copy-done.4
  28.7 0.9 fusion.74
  29.8 0.5 neg.19
  30.3 88.0 %all-reduce.3.cloned.1.call-done = f32[32,512]{1,0:T(8,128)} async-done(((f32[32,512]{1,0:T(8,128)}), f32[32,512]{1,0:T(8,128)}) %all-reduce.3.cloned.1.call-update) | async-done | bytes 65552 | tf_op jit(solution)/shard_map/psum | solution.py:100
  118.3 1.0 multiply_reduce_fusion.8
  119.3 0.5 add_sqrt_fusion.2
  119.8 55.7 %all-gather.3.cloned.1.call-done = bf16[2048,2048]{1,0:T(8,128)(2,1)} async-done(((bf16[128,2048]{1,0:T(8,128)(2,1)}), bf16[2048,2048]{1,0:T(8,128)(2,1)}) %all-gather.3.cloned.1.call-update) | async-done | bytes 8388624 | tf_op jit(solution)/shard_map/all_gather | solution.py:115
  175.5 6.4 convolution_bitcast_fusion.1
  182.1 1.6 fusion.32
  183.9 2.7 convert_reduce_fusion.1
  186.6 2.1 fusion.37
  188.8 47.4 %psum.21 = f32[16,512]{1,0:T(8,128)} all-reduce(f32[16,512]{1,0:T(8,128)S(1)} %fusion.59), channel_id=1, replica_groups=mesh['sec'=2,'dp'=8,'seq'=16] {'seq'}, use_global_device_ids=true, to_apply=%region_10.11 | all-reduce | flops 8192 | bytes 65536 | tf_op jit(solution)/shard_map/psum | solution.py:139
  236.2 1.2 multiply_reduce_fusion.9
  237.5 1.0 fusion.45
  238.4 0.4 multiply_convert_fusion
  238.8 1.7 fusion.35
  241.0 0.6 convolution_bitcast_fusion.2
  241.5 1.0 copy-done.2
  242.7 0.8 multiply_reduce_fusion.1
  243.4 0.6 divide_convert_fusion.1
  244.0 0.8 copy-done.9
  244.8 8.1 %convolution_bitcast_fusion = f32[16,128,2048]{2,1,0:T(8,128)} fusion(bf16[16,128,1,128]{1,3,0,2:T(8,128)(2,1)S(1)} %multiply_convert_fusion, bf16[16,128,1,128]{1,3,0,2:T(8,128)(2,1)S(1)} %get-tuple-element.60, bf16[16,128,1,128]{1,3,0,2:T(8,128)(2,1)S(1)} %get-tuple-element.59, bf16[3,2048,128]{2,1,0:T(8,128)(2,1)S(1)} %copy-done.9), kind=kOutput, calls=%fused_computation.2 | convolution fusion | flops 3222798336 | bytes 19922944 | tf_op jit(solution)/shard_map/cfjk,jdk->cfd/dot_general | solution.py:182
  253.2 100.2 %reduce-scatter.2.cloned.1.call-done = f32[1,128,2048]{2,1,0:T(8,128)} async-done(((f32[16,128,2048]{2,1,0:T(8,128)}), f32[1,128,2048]{2,1,0:T(8,128)}) %reduce-scatter.2.cloned.1.call-update) | async-done | bytes 1048592 | tf_op jit(solution)/shard_map/reduce_scatter | solution.py:181
  353.5 1.9 fusion.30
  355.7 2.1 multiply_reduce_fusion.7
  358.4 2.0 fusion.66
  360.8 2.7 fusion.27
  363.6 1.3 fusion.40
  364.9 1.0 scatter-add.10
  367.2 3.3 fusion.53
  370.5 0.7 copy-done.15
  371.2 3.2 fusion.18
  374.3 1.5 reduce_sum.224
  375.8 2.8 fusion.21
  378.7 253.5 %all-reduce.5.cloned.1.call-done = f32[2560,256]{1,0:T(8,128)} async-done(((f32[2560,256]{1,0:T(8,128)}), f32[2560,256]{1,0:T(8,128)}) %all-reduce.5.cloned.1.call-update) | async-done | bytes 2621456 | tf_op jit(solution)/shard_map/psum | solution.py:201
  632.2 1.6 constant_dynamic-slice_fusion
  (110 shorter events, 5.8 us)
Async XLA Ops:
  7.2 1.9 copy-start
  7.2 111.1 %all-reduce.3.cloned.1.call-start = ((), (), s32[]{:S(2)}) async-start(), calls=%async_computation.1 | async-start | bytes 131072 | tf_op jit(solution)/shard_map/psum | solution.py:100
  14.1 5.8 copy-start.20
  14.1 6.4 %copy-start.21 = (bf16[1,2560]{1,0:T(2,128)(2,1)S(1)}, bf16[1,2560]{1,0:T(2,128)(2,1)}, u32[]{:S(2)}) copy-start(bf16[1,2560]{1,0:T(2,128)(2,1)} %param.21) | copy-start | bytes 15364
  14.1 6.4 %copy-start.22 = (bf16[1,2560]{1,0:T(2,128)(2,1)S(1)}, bf16[1,2560]{1,0:T(2,128)(2,1)}, u32[]{:S(2)}) copy-start(bf16[1,2560]{1,0:T(2,128)(2,1)} %param.22) | copy-start | bytes 15364
  14.2 6.5 %copy-start.36 = (bf16[1,128,256]{2,1,0:T(8,128)(2,1)S(1)}, bf16[1,128,256]{2,1,0:T(8,128)(2,1)}, u32[]{:S(2)}) copy-start(bf16[1,128,256]{2,1,0:T(8,128)(2,1)} %param.23) | copy-start | bytes 196612
  16.5 159.0 %all-gather.3.cloned.1.call-start = ((), (), s32[]{:S(2)}) async-start(), calls=%async_computation.4 | async-start | bytes 8912896 | tf_op jit(solution)/shard_map/all_gather | solution.py:115
  16.5 4.1 copy-start.3
  18.5 3.9 copy-start.23
  20.0 2.5 copy-start.27
  20.7 1.8 copy-start.14
  20.7 1.8 copy-start.17
  23.3 0.6 copy-start.31
  23.8 0.5 copy-start.33
  24.9 2.8 copy-start.10
  27.7 1.0 copy-start.4
  27.8 2.0 copy-start.37
  27.8 1.0 copy-start.25
  29.7 323.8 %reduce-scatter.2.cloned.1.call-start = ((), (), s32[]{:S(2)}) async-start(), calls=%async_computation.2 | async-start | bytes 17825792 | tf_op jit(solution)/shard_map/reduce_scatter | solution.py:181
  181.9 2.0 copy-start.1
  183.9 4.8 copy-start.13
  183.9 52.3 %copy-start.16 = (f32[32,512]{1,0:T(8,128)S(1)}, f32[32,512]{1,0:T(8,128)}, u32[]{:S(2)}) copy-start(f32[32,512]{1,0:T(8,128)} %all-reduce.3.cloned.1.call-done) | copy-start | bytes 196612
  236.2 4.4 copy-start.6
  237.4 3.5 copy-start.35
  238.4 2.5 copy-start.8
  240.6 1.9 copy-start.2
  241.0 1.7 copy-start.12
  243.4 1.4 copy-start.9
  253.0 100.5 %copy-start.26 = (f32[128]{0:T(128)S(1)}, f32[128]{0:T(128)}, u32[]{:S(2)}) copy-start(f32[128]{0:T(128)} %copy-done.25) | copy-start | bytes 1540
  253.0 102.5 %copy-start.19 = (f32[1,2048]{1,0:T(1,128)S(1)}, f32[1,2048]{1,0:T(1,128)}, u32[]{:S(2)}) copy-start(f32[1,2048]{1,0:T(1,128)} %get-tuple-element.67) | copy-start | bytes 24580
  253.0 102.5 %copy-start.18 = (f32[1,2048]{1,0:T(1,128)S(1)}, f32[1,2048]{1,0:T(1,128)}, u32[]{:S(2)}) copy-start(f32[1,2048]{1,0:T(1,128)} %get-tuple-element.66) | copy-start | bytes 24580
  253.0 379.2 %all-reduce.5.cloned.1.call-start = ((), (), s32[]{:S(2)}) async-start(), calls=%async_computation.3 | async-start | bytes 5242880 | tf_op jit(solution)/shard_map/psum | solution.py:201
  353.5 2.0 copy-start.5
  353.5 2.2 copy-start.7
  355.6 2.7 copy-start.29
  355.6 2.7 copy-start.30
  355.6 2.7 copy-start.32
  355.6 2.7 copy-start.34
  355.6 5.0 copy-start.11
  370.5 0.7 copy-start.15
  370.5 0.7 copy-start.24
  370.5 0.7 copy-start.28
Sparse Core Ops, SparseCore 0:
  16.6 101.6 all-reduce.2
  120.9 54.6 all-gather.2
  253.1 100.3 reduce-scatter.1
  370.6 261.4 all-reduce.4
where the time goes:
time: 641 us; the launch traced here: 640 us
  waiting for transfers between devices  498 us (78%)
  blocking collectives  47.4 us (7%)
  matrix products  37.3 us (6%)
  other arithmetic  26.9 us (4%)
  local copies, waits for them, and re-layouts  15.9 us (2%)
  between operations  14.9 us (2%)
    psum x1, waiting for transfers between devices, local(): grad_total = lax.psum(grad_term, ('sec', 'dp', 'seq'))  253 us
    reduce_scatter x1, waiting for transfers between devices, local(): lax.psum_scatter(jnp.einsum('cfjk,jdk->cfd', d_proj, w_qkv, preferred_ele...  100 us
    psum x1, waiting for transfers between devices, local(): text_raw = lax.psum(text_part, 'seq')  88 us
    all_gather x1, waiting for transfers between devices, local(): lax.all_gather(normed_e.astype(jnp.bfloat16), 'seq', axis=0, tiled=True)  55.7 us
    psum x1, blocking collectives, local(): motion_emb = lax.psum(motion_part, 'seq')  47.4 us
  transfers between devices with their start and end apart: 4, of which 4 were waited for; matrix products, arithmetic and copies ran while one was open for 3% of the time, Pallas kernels for 0%

commit v1 on v0

--- a/solution.py
+++ b/solution.py
@@ -9,6 +9,12 @@
 normalizing_sharpness = 10.0
 epsilon = 1e-06
 highest = lax.Precision.HIGHEST
+
+
+def open_map_on_mesh(row_data, named_axis, array_dim=0):
+    back = jnp.stack(jax.lax.psum(1, named_axis) * [row_data])
+    v_next = jax.lax.all_to_all(back, named_axis, 0, 0)
+    return jnp.concatenate(v_next, axis=array_dim)
 
 
 def rotate(angle, first, second):
@@ -112,7 +118,7 @@
     normed_e, scale_rms = embed(x_clean, path_east, path_north, w_embed, root_rows)
     projected = jnp.einsum(
         "cfd,jdk->cfjk",
-        lax.all_gather(normed_e.astype(jnp.bfloat16), "seq", axis=0, tiled=True),
+        open_map_on_mesh(normed_e.astype(jnp.bfloat16), "seq"),
         w_qkv,
         preferred_element_type=jnp.float32,
     )

time: 641 us -> 695 us (1.084)
  waiting for transfers between devices: 498 us -> 542 us
  starting transfers between devices: 0.34 us -> 8.88 us
    psum x1, waiting for transfers between devices: 88 us -> 187 us  [local(): text_raw = lax.psum(text_part, 'seq')]
    all_gather x1 -> x0, waiting for transfers between devices: 55.7 us -> none  [local(): lax.all_gather(normed_e.astype(jnp.bfloat16), 'seq', axis=0, tiled=True)]
    all_to_all x0 -> x1, starting transfers between devices: none -> 8.75 us  [open_map_on_mesh(): v_next = jax.lax.all_to_all(back, named_axis, 0, 0)]
  transfers between devices with their start and end apart: 4 -> 4, of which waited for: 4 -> 3; matrix products, arithmetic and copies ran while one was open for 3% -> 2% of each run, Pallas kernels for 0% -> 0%
where the time goes in v1:
time: 695 us; the launch traced here: 694 us
  waiting for transfers between devices  542 us (78%)
  blocking collectives  46.5 us (7%)
  matrix products  37.3 us (5%)
  other arithmetic  25.3 us (4%)
  local copies, waits for them, and re-layouts  19.3 us (3%)
  between operations  15.1 us (2%)
  starting transfers between devices  8.88 us (1%)
    psum x1, waiting for transfers between devices, local(): grad_total = lax.psum(grad_term, ('sec', 'dp', 'seq'))  253 us
    psum x1, waiting for transfers between devices, local(): text_raw = lax.psum(text_part, 'seq')  187 us
    reduce_scatter x1, waiting for transfers between devices, local(): lax.psum_scatter(jnp.einsum('cfjk,jdk->cfd', d_proj, w_qkv, preferred_ele...  101 us
    psum x1, blocking collectives, local(): motion_emb = lax.psum(motion_part, 'seq')  46.5 us
  transfers between devices with their start and end apart: 4, of which 3 were waited for; matrix products, arithmetic and copies ran while one was open for 2% of the time, Pallas kernels for 0%

profile of v1, /device:TPU:2, one launch (start us, length us, event | category | flops | bytes accessed | tf_op | source)
XLA Modules:
  0.0 694.0 jit_solution(10752710417186494003)
XLA Ops:
  8.0 1.4 convert_reduce_fusion
  9.4 1.4 fusion.27
  10.8 0.6 fusion.82
  11.6 1.8 fusion.29
  13.4 0.8 slice_reduce_fusion.1
  14.7 0.5 copy-done.34
  16.0 0.6 subtract_reduce_fusion.1
  16.9 1.7 multiply_reduce_fusion.3
  18.6 1.0 copy-done.4
  19.8 4.3 stack.4
  24.0 8.8 %all-to-all-start = ((bf16[16,1,128,2048]{3,2,1,0:T(8,128)(2,1)}), bf16[16,1,128,2048]{3,2,1,0:T(8,128)(2,1)}, u32[]{:S(2)}, u32[]{:S(2)}) async-start(bf16[16,1,128,2048]{3,2,1,0:T(8,128)(2,1)} %stack.4), calls=%async_computation | async-start | bytes 16777216 | tf_op jit(solution)/shard_map/all_to_all | solution.py:16
  33.0 5.1 gather_fusion
  38.0 2.2 select_reduce_fusion
  40.4 0.5 neg.19
  40.9 186.8 %all-reduce.3.cloned.1.call-done = f32[32,512]{1,0:T(8,128)} async-done(((f32[32,512]{1,0:T(8,128)}), f32[32,512]{1,0:T(8,128)}) %all-reduce.3.cloned.1.call-update) | async-done | bytes 65552 | tf_op jit(solution)/shard_map/psum | solution.py:106
  227.7 1.0 multiply_reduce_fusion.8
  228.7 0.5 add_sqrt_fusion.2
  229.2 6.4 fusion.4
  235.8 1.6 fusion.37
  237.6 2.7 convert_reduce_fusion.1
  240.3 2.1 fusion.42
  242.5 46.5 %psum.21 = f32[16,512]{1,0:T(8,128)} all-reduce(f32[16,512]{1,0:T(8,128)S(1)} %fusion.64), channel_id=1, replica_groups=mesh['sec'=2,'dp'=8,'seq'=16] {'seq'}, use_global_device_ids=true, to_apply=%region_10.11 | all-reduce | flops 8192 | bytes 65536 | tf_op jit(solution)/shard_map/psum | solution.py:145
  289.0 1.2 multiply_reduce_fusion.9
  290.3 1.0 fusion.50
  291.2 0.4 multiply_convert_fusion
  291.6 1.7 fusion.40
  293.8 0.6 convolution_bitcast_fusion.1
  294.3 1.0 copy-done.2
  295.5 0.8 multiply_reduce_fusion.1
  296.2 0.6 divide_convert_fusion.1
  296.8 0.8 copy-done.9
  297.6 8.1 %convolution_bitcast_fusion = f32[16,128,2048]{2,1,0:T(8,128)} fusion(bf16[16,128,1,128]{1,3,0,2:T(8,128)(2,1)S(1)} %multiply_convert_fusion, bf16[16,128,1,128]{1,3,0,2:T(8,128)(2,1)S(1)} %get-tuple-element.60, bf16[16,128,1,128]{1,3,0,2:T(8,128)(2,1)S(1)} %get-tuple-element.59, bf16[3,2048,128]{2,1,0:T(8,128)(2,1)S(1)} %copy-done.9), kind=kOutput, calls=%fused_computation.4 | convolution fusion | flops 3222798336 | bytes 19922944 | tf_op jit(solution)/shard_map/cfjk,jdk->cfd/dot_general | solution.py:188
  305.8 101.4 %reduce-scatter.2.cloned.1.call-done = f32[1,128,2048]{2,1,0:T(8,128)} async-done(((f32[16,128,2048]{2,1,0:T(8,128)}), f32[1,128,2048]{2,1,0:T(8,128)}) %reduce-scatter.2.cloned.1.call-update) | async-done | bytes 1048592 | tf_op jit(solution)/shard_map/reduce_scatter | solution.py:187
  407.3 1.9 fusion.35
  409.4 2.1 multiply_reduce_fusion.7
  412.2 2.0 fusion.71
  414.6 2.7 fusion.32
  417.4 1.3 fusion.45
  418.7 1.0 scatter-add.10
  420.0 0.4 scatter-add.11
  420.6 0.4 scatter-add.14
  421.0 3.3 fusion.58
  424.3 0.7 copy-done.15
  425.0 3.2 fusion.23
  428.1 1.5 reduce_sum.224
  429.6 2.8 fusion.26
  432.4 253.4 %all-reduce.5.cloned.1.call-done = f32[2560,256]{1,0:T(8,128)} async-done(((f32[2560,256]{1,0:T(8,128)}), f32[2560,256]{1,0:T(8,128)}) %all-reduce.5.cloned.1.call-update) | async-done | bytes 2621456 | tf_op jit(solution)/shard_map/psum | solution.py:207
  685.9 1.6 constant_dynamic-slice_fusion
  (112 shorter events, 5.0 us)
Async XLA Ops:
  7.2 25.8 %copy-start = (bf16[3088,512]{1,0:T(8,128)(2,1)S(1)}, bf16[3088,512]{1,0:T(8,128)(2,1)}, u32[]{:S(2)}) copy-start(bf16[3088,512]{1,0:T(8,128)(2,1)} %param.30) | copy-start | bytes 9486340
  7.2 4.4 copy-start.3
  7.2 3.6 copy-start.20
  7.2 4.2 copy-start.23
  7.2 4.2 copy-start.22
  7.2 4.3 copy-start.37
  9.4 3.9 copy-start.24
  10.8 2.5 copy-start.28
  11.5 1.8 copy-start.14
  11.5 1.8 copy-start.17
  14.1 0.6 copy-start.32
  14.7 0.5 copy-start.34
  15.8 2.8 copy-start.10
  18.6 1.0 copy-start.4
  18.6 1.1 copy-start.26
  24.0 8.8 %copy-start.21 = (s32[32,32]{1,0:T(8,128)S(1)}, s32[32,32]{1,0:T(8,128)}, u32[]{:S(2)}) copy-start(s32[32,32]{1,0:T(8,128)} %param.31) | copy-start | bytes 12292
  24.0 205.2 %all-to-all-start = ((bf16[16,1,128,2048]{3,2,1,0:T(8,128)(2,1)}), bf16[16,1,128,2048]{3,2,1,0:T(8,128)(2,1)}, u32[]{:S(2)}, u32[]{:S(2)}) async-start(bf16[16,1,128,2048]{3,2,1,0:T(8,128)(2,1)} %stack.4), calls=%async_computation | async-start | bytes 16777216 | tf_op jit(solution)/shard_map/all_to_all | solution.py:16
  32.8 194.9 %all-reduce.3.cloned.1.call-start = ((), (), s32[]{:S(2)}) async-start(), calls=%async_computation.2 | async-start | bytes 131072 | tf_op jit(solution)/shard_map/psum | solution.py:106
  33.0 7.4 %copy-start.38 = (f32[16]{0:T(128)S(1)}, f32[16]{0:T(128)}, u32[]{:S(2)}) copy-start(f32[16]{0:T(128)} %param.33) | copy-start | bytes 196
  40.3 366.9 %reduce-scatter.2.cloned.1.call-start = ((), (), s32[]{:S(2)}) async-start(), calls=%async_computation.3 | async-start | bytes 17825792 | tf_op jit(solution)/shard_map/reduce_scatter | solution.py:187
  235.6 2.0 copy-start.1
  237.6 4.8 copy-start.13
  237.6 51.4 %copy-start.16 = (f32[32,512]{1,0:T(8,128)S(1)}, f32[32,512]{1,0:T(8,128)}, u32[]{:S(2)}) copy-start(f32[32,512]{1,0:T(8,128)} %all-reduce.3.cloned.1.call-done) | copy-start | bytes 196612
  289.0 4.4 copy-start.6
  290.2 3.5 copy-start.36
  291.2 2.5 copy-start.8
  293.4 1.9 copy-start.2
  293.8 1.7 copy-start.12
  296.2 1.4 copy-start.9
  305.8 101.5 %copy-start.27 = (f32[128]{0:T(128)S(1)}, f32[128]{0:T(128)}, u32[]{:S(2)}) copy-start(f32[128]{0:T(128)} %copy-done.26) | copy-start | bytes 1540
  305.8 103.5 %copy-start.19 = (f32[1,2048]{1,0:T(1,128)S(1)}, f32[1,2048]{1,0:T(1,128)}, u32[]{:S(2)}) copy-start(f32[1,2048]{1,0:T(1,128)} %get-tuple-element.67) | copy-start | bytes 24580
  305.8 103.4 %copy-start.18 = (f32[1,2048]{1,0:T(1,128)S(1)}, f32[1,2048]{1,0:T(1,128)}, u32[]{:S(2)}) copy-start(f32[1,2048]{1,0:T(1,128)} %get-tuple-element.66) | copy-start | bytes 24580
  305.8 380.1 %all-reduce.5.cloned.1.call-start = ((), (), s32[]{:S(2)}) async-start(), calls=%async_computation.4 | async-start | bytes 5242880 | tf_op jit(solution)/shard_map/psum | solution.py:207
  407.3 2.0 copy-start.5
  407.3 2.2 copy-start.7
  409.4 2.7 copy-start.30
  409.4 2.7 copy-start.31
  409.4 2.7 copy-start.33
  409.4 2.7 copy-start.35
  409.4 5.0 copy-start.11
  424.3 0.7 copy-start.15
  424.3 0.7 copy-start.25
  424.3 0.7 copy-start.29
Sparse Core Ops, SparseCore 0:
  40.4 187.2 all-reduce.2
  305.9 101.2 reduce-scatter.1
  424.4 261.4 all-reduce.4
